TPU v7x, 256 devices: a whole 4x4x8 slice. The times are simulated.
256 devices in a mesh: grid: 16 (over y_hi, z), states: 16 (over y_lo, x, core).
Axes of the slice: x: 4, y: 4 (y_hi: 2, y_lo: 2; y = y_hi * 2 + y_lo), z: 8, core: 2. Of those that a mesh axis runs over, the one named last changes fastest.
Arguments:
- states_in: float32 [16, 256, 32, 128], P('states', 'grid'), may hold values from -10 to 10
- potential: float32 [256, 32, 128], P('grid'), may hold values from -2 to 0.5
- projectors: bfloat16 [16, 32, 8, 4096], P('grid', 'states'), may hold values from -0.0625 to 0.0625
- proj_gains: bfloat16 [16, 32, 8], P('grid', 'states'), may hold values from 1 to 6
- atom_owner: int32 [160], P('grid'), may hold values from 0 to 15, as said below
- atom_rows: int32 [160, 32], P('grid'), may hold values from -1 to 8191, as said below
- wrap_rows: int32 [32], replicated, may hold values from 0 to 31, as said below
Outputs:
- filtered: float32 [16, 256, 32, 128], P('states', 'grid')
Inputs may be any that keep to these rules, and one draw needn't show every extreme that they name: `atom_owner`: atom a belongs to tile a // 10. At most 2 atoms of one tile share an owner, and one owner takes exactly 2 atoms of every tile. `atom_rows`: A row r is the line of cells at x = r // 32, y = r % 32. Each list holds distinct rows whose x lies in the atom's own tile of 16 planes, followed by -1 entries; each list has 16 rows or more, and the first atom of every tile fills all 32. wrap_rows[y] = (y + t) mod 32 for one t of 1 to 31.
All inputs are finite; a program needn't handle non-finite values.
Results may differ from a plain program's by a relative error of at most 0.00082.
Values may be sent and summed in bfloat16 or wider, within the bound.
No kernel may reach another device: no remote copies, remote signals or barrier semaphores. Data moves between devices by JAX's collectives and lax.ppermute only.
A program may use at most 64 MiB of HBM per device.

v0:
```python
import math
import jax
import jax.numpy as jnp
from jax import lax
from jax.sharding import PartitionSpec as P

RADIUS = 6
PAIR_CAP = 2
MIXED_WEIGHT = 0.7
CENTER = 12.0
HALF_WIDTH = 8.0


def padded_2(shard, sides, width):
    for axis, dim in sides:
        count, length = (lax.axis_size(axis), shard.shape[dim])
        up = [(i, (i + 1) % count) for i in range(count)]
        down = [(j, i) for i, j in up]
        last = lax.slice_in_dim(shard, length - width, length, axis=dim)
        initial = lax.slice_in_dim(shard, 0, width, axis=dim)
        before = lax.ppermute(last, axis, up)
        after = lax.ppermute(initial, axis, down)
        shard = jnp.concatenate([before, shard, after], axis=dim)
    return shard


def second_table(radius):
    weights = [-2.0 * sum((1.0 / (k * k) for k in range(1, radius + 1)))]
    for k in range(1, radius + 1):
        weights.append(
            2.0
            * (-1) ** (k + 1)
            * math.factorial(radius) ** 2
            / (k * k * math.factorial(radius - k) * math.factorial(radius + k))
        )
    return weights


def first_table(radius):
    weights = [0.0]
    for k in range(1, radius + 1):
        weights.append(
            (-1) ** (k + 1)
            * math.factorial(radius) ** 2
            / (k * math.factorial(radius - k) * math.factorial(radius + k))
        )
    return weights


def laplacian(padded, plane_count):
    second_weights = second_table(RADIUS)
    first_weights = first_table(RADIUS)
    interior = padded[:, RADIUS : RADIUS + plane_count]
    line_depth = interior.shape[3]
    z_padded = jnp.pad(interior, ((0, 0), (0, 0), (0, 0), (RADIUS, RADIUS)))
    summed = 3.0 * second_weights[0] * interior
    y_slope = jnp.zeros_like(padded)
    for k in range(1, RADIUS + 1):
        summed = summed + second_weights[k] * (
            padded[:, RADIUS + k : RADIUS + k + plane_count]
            + padded[:, RADIUS - k : RADIUS - k + plane_count]
        )
        summed = summed + second_weights[k] * (jnp.roll(interior, -k, 2) + jnp.roll(interior, k, 2))
        summed = summed + second_weights[k] * (
            z_padded[:, :, :, RADIUS + k : RADIUS + k + line_depth]
            + z_padded[:, :, :, RADIUS - k : RADIUS - k + line_depth]
        )
        y_slope = y_slope + first_weights[k] * (jnp.roll(padded, -k, 2) - jnp.roll(padded, k, 2))
    cross_term = jnp.zeros_like(interior)
    for k in range(1, RADIUS + 1):
        cross_term = cross_term + first_weights[k] * (
            y_slope[:, RADIUS + k : RADIUS + k + plane_count]
            - y_slope[:, RADIUS - k : RADIUS - k + plane_count]
        )
    return summed + MIXED_WEIGHT * cross_term


def shards(states_in, potential, projectors, proj_gains, atom_owner, atom_rows, wrap_rows):
    state_count, tile_width, breadth, line_depth = states_in.shape
    n_grid = lax.axis_size("grid")
    tile_index = lax.axis_index("grid")
    tile_lines = tile_width * breadth
    block_rows = atom_rows.shape[1]
    line_span = block_rows * line_depth
    proj_count = projectors.shape[2]
    home_count = atom_owner.shape[0]
    row_order = jnp.arange(breadth, dtype=jnp.int32)
    unwrap_rows = jnp.sum(
        row_order[None, :] * (wrap_rows[None, :] == row_order[:, None]).astype(jnp.int32), axis=1
    )
    atom_order = jnp.arange(home_count, dtype=jnp.int32)
    same_owner = (atom_owner[:, None] == atom_owner[None, :]) & (
        atom_order[None, :] < atom_order[:, None]
    )
    owner_rank = jnp.sum(same_owner.astype(jnp.int32), axis=1)
    atom_slot = atom_owner * PAIR_CAP + owner_rank
    local_rows = jnp.where(atom_rows >= 0, atom_rows - tile_index * tile_lines, tile_lines)
    full_proj, full_gain = (
        lax.all_gather(projectors, "states", axis=1, tiled=True),
        lax.all_gather(proj_gains, "states", axis=1, tiled=True),
    )
    full_proj = full_proj.reshape(n_grid, PAIR_CAP, proj_count, line_span)
    full_gain = full_gain.reshape(n_grid, PAIR_CAP, proj_count)

    def extended(grid_field):
        padded = padded_2(grid_field, (("grid", 1),), RADIUS)
        low_rim = padded[:, :RADIUS]
        high_rim = padded[:, RADIUS + tile_width :]
        low_rim = jnp.where(tile_index == 0, jnp.take(low_rim, wrap_rows, axis=2), low_rim)
        high_rim = jnp.where(
            tile_index == n_grid - 1, jnp.take(high_rim, unwrap_rows, axis=2), high_rim
        )
        return jnp.concatenate([low_rim, padded[:, RADIUS : RADIUS + tile_width], high_rim], axis=1)

    def pick_rows(grid_field):
        lines_here = grid_field.reshape(state_count, tile_lines, line_depth)
        picked = jnp.take(lines_here, local_rows, axis=1, mode="fill", fill_value=0.0).astype(
            jnp.bfloat16
        )
        return jnp.swapaxes(picked.reshape(state_count, home_count, line_span), 0, 1)

    def place_rows(projected):
        pieces = (
            jnp.swapaxes(projected, 0, 1)
            .reshape(state_count, home_count, block_rows, line_depth)
            .astype(jnp.float32)
        )
        summed = (
            jnp.zeros((state_count, tile_lines, line_depth), jnp.float32)
            .at[:, local_rows]
            .add(pieces, mode="drop")
        )
        return summed.reshape(state_count, tile_width, breadth, line_depth)

    def at_owner(received):
        coefficients = jnp.einsum(
            "gpjc,gpsc->gpsj", full_proj, received, preferred_element_type=jnp.float32
        )
        scaled = (coefficients * full_gain[:, :, None, :].astype(jnp.float32)).astype(jnp.bfloat16)
        projected = jnp.einsum(
            "gpjc,gpsj->gpsc", full_proj, scaled, preferred_element_type=jnp.float32
        ).astype(jnp.bfloat16)
        return lax.all_to_all(projected, "grid", split_axis=0, concat_axis=0, tiled=True)

    def nonlocal_part(grid_field):
        picked = pick_rows(grid_field)
        outbox = (
            jnp.zeros((n_grid * PAIR_CAP, state_count, line_span), jnp.bfloat16)
            .at[atom_slot]
            .set(picked)
        )
        outbox = outbox.reshape(n_grid, PAIR_CAP, state_count, line_span)
        returned_rows = at_owner(
            lax.all_to_all(outbox, "grid", split_axis=0, concat_axis=0, tiled=True)
        )
        projected = jnp.take(
            returned_rows.reshape(n_grid * PAIR_CAP, state_count, line_span), atom_slot, axis=0
        )
        return place_rows(projected)

    def operate(grid_field):
        padded = extended(grid_field)
        return (
            -0.5 * laplacian(padded, tile_width)
            + potential[None] * grid_field
            + nonlocal_part(grid_field)
        )

    def shifted(grid_field):
        return (operate(grid_field) - CENTER * grid_field) / HALF_WIDTH

    first_term = shifted(states_in)
    second_term = 2.0 * shifted(first_term) - states_in
    return 2.0 * shifted(second_term) - first_term


def solution(mesh):
    in_specs = (
        P("states", "grid", None, None),
        P("grid", None, None),
        P("grid", "states", None, None),
        P("grid", "states", None),
        P("grid"),
        P("grid", None),
        P(),
    )
    out_specs = P("states", "grid", None, None)
    return jax.shard_map(shards, mesh=mesh, in_specs=in_specs, out_specs=out_specs, check_vma=False)
```

profile of v0, /device:TPU:32, one launch (start us, length us, event | category | flops | bytes accessed | tf_op | source)
XLA Modules:
  0.0 244.3 jit_solution(14710537106557358727)
XLA Ops:
  6.5 1.1 copy.128
  7.7 1.9 collective-permute-start
  11.1 2.1 gather_fusion.2
  15.9 13.5 %all-to-all-start = ((bf16[16,2,1,4096]{3,1,2,0:T(2,128)(2,1)}), bf16[16,2,1,4096]{3,1,2,0:T(2,128)(2,1)S(1)}, u32[]{:S(2)}, u32[]{:S(2)}) async-start(bf16[16,2,1,4096]{3,1,2,0:T(2,128)(2,1)} %reshape.2251), calls=%async_computation | async-start | bytes 524288 | tf_op jit(solution)/shard_map/all_to_all | solution.py:154
  36.3 18.8 %all_gather.7 = bf16[1,32,8]{2,0,1:T(2,128)(2,1)S(1)} all-gather(bf16[1,2,8]{2,0,1:T(2,128)(2,1)S(1)} %copy.162), channel_id=1, replica_groups=mesh['grid'=16,'states'=16] {'states'}, dimensions={1}, use_global_device_ids=true | all-gather | bytes 544 | tf_op jit(solution)/shard_map/all_gather | solution.py:100
  61.3 1.1 fusion.338
  64.5 1.1 fusion.344
  65.6 1.1 fusion.346
  66.6 3.0 %all-gather.2.cloned.1.call-done = bf16[1,32,8,4096]{3,2,0,1:T(8,128)(2,1)} async-done(((bf16[1,2,8,4096]{3,2,0,1:T(8,128)(2,1)}), bf16[1,32,8,4096]{3,2,0,1:T(8,128)(2,1)}) %all-gather.2.cloned.1.call-update) | async-done | bytes 2097168 | tf_op jit(solution)/shard_map/all_gather | solution.py:99
  69.6 3.3 %fusion.46 = f32[16,2,1,8]{3,2,1,0:T(1,128)S(1)} fusion(bf16[16,2,8,4096]{3,2,1,0:T(8,128)(2,1)} %bitcast.158, bf16[16,2,4096,1]{2,1,0,3:T(2,128)(2,1)} %bitcast.182), kind=kOutput, calls=%fused_computation.193 | convolution fusion | flops 2097152 | bytes 2360320 | tf_op jit(solution)/shard_map/gpjc,gpsc->gpsj/dot_general | solution.py:136
  73.6 1.1 copy.216
  74.7 9.6 %all-to-all-start.1 = ((bf16[16,2,1,4096]{3,1,2,0:T(2,128)(2,1)}), bf16[16,2,1,4096]{3,1,2,0:T(2,128)(2,1)}, u32[]{:S(2)}, u32[]{:S(2)}) async-start(bf16[16,2,1,4096]{3,1,2,0:T(2,128)(2,1)} %bitcast.153), calls=%async_computation.1 | async-start | bytes 524288 | tf_op jit(solution)/shard_map/all_to_all | solution.py:143
  85.8 2.5 %fusion.25 = f32[1,28,32,128]{3,1,2,0:T(8,128)S(1)} fusion(f32[1,6,32,128]{3,1,2,0:T(8,128)S(1)} %fusion.285, f32[1,16,32,128]{3,1,2,0:T(8,128)S(1)} %copy.128, f32[1,6,32,128]{3,1,2,0:T(8,128)S(1)} %fusion.284, f32[1,28,31,128]{3,1,2,0:T(8,128)S(1)} %get-tuple-element.79, f32[1,28,31,128]{3,1,2,0:T(8,128)S(1)} %get-tuple-element.78, ...), kind=kLoop, calls=%fused_computation.148 | loop fusion | flops 3784704 | bytes 6393856 | tf_op jit(solution)/shard_map/add | solution.py:68
  88.2 8.2 %all-to-all-done.1 = bf16[16,2,1,4096]{3,1,2,0:T(2,128)(2,1)} async-done(((bf16[16,2,1,4096]{3,1,2,0:T(2,128)(2,1)}), bf16[16,2,1,4096]{3,1,2,0:T(2,128)(2,1)}, u32[]{:S(2)}, u32[]{:S(2)}) %all-to-all-start.1) | async-done | bytes 262176 | tf_op jit(solution)/shard_map/all_to_all | solution.py:143
  96.4 1.0 reshape.2505
  97.5 1.4 gather_fusion.3
  100.6 2.7 %scatter_custom_fusion.1 = f32[512,128]{1,0:T(8,128)} fusion(s32[320]{0:T(512)} %copy-done.43, f32[320,128]{1,0:T(8,128)} %reshape.2406, f32[]{:T(128)} %constant.58.clone.1), kind=kCustom, calls=%fused_computation.503 | custom fusion | flops 40960 | bytes 262656 | tf_op jit(solution)/shard_map/scatter-add | solution.py:131
  103.2 4.3 %broadcast_multiply_fusion = (f32[1,16,32,128]{3,1,2,0:T(8,128)S(1)}, f32[1,16,32,128]{3,1,2,0:T(8,128)}) fusion(f32[1,16,32,128]{3,1,2,0:T(8,128)S(1)} %copy.128, f32[1,16,32,128]{3,2,1,0:T(8,128)} %bitcast.168, f32[16,32,128]{2,1,0:T(8,128)S(1)} %copy-done.2, f32[1,28,32,128]{3,1,2,0:T(8,128)S(1)} %fusion.25, f32[1,16,26,128]{3,1,2,0:T(8,128)} %get-tuple-element.153, ...), kind=kLoop, calls=%fused_computation.505 | loop fusion | flops 6881280 | bytes 7798784 | tf_op jit(solution)/shard_map/div | solution.py:170
  115.9 1.9 collective-permute-start.3
  117.8 1.4 gather_fusion.6
  121.9 7.9 %all-to-all-start.2 = ((bf16[16,2,1,4096]{3,1,2,0:T(2,128)(2,1)}), bf16[16,2,1,4096]{3,1,2,0:T(2,128)(2,1)}, u32[]{:S(2)}, u32[]{:S(2)}) async-start(bf16[16,2,1,4096]{3,1,2,0:T(2,128)(2,1)} %reshape.2257), calls=%async_computation.2 | async-start | bytes 524288 | tf_op jit(solution)/shard_map/all_to_all | solution.py:154
  131.6 1.1 fusion.333
  132.7 1.0 fusion.331
  133.7 1.0 fusion.329
  137.1 1.1 fusion.335
  138.2 2.3 all-to-all-done.2
  140.5 2.4 fusion.44
  143.6 1.1 copy.217
  144.7 7.3 %all-to-all-start.3 = ((bf16[16,2,1,4096]{3,1,2,0:T(2,128)(2,1)}), bf16[16,2,1,4096]{3,1,2,0:T(2,128)(2,1)}, u32[]{:S(2)}, u32[]{:S(2)}) async-start(bf16[16,2,1,4096]{3,1,2,0:T(2,128)(2,1)} %bitcast.155), calls=%async_computation.3 | async-start | bytes 524288 | tf_op jit(solution)/shard_map/all_to_all | solution.py:143
  153.5 2.5 %fusion.16 = f32[1,28,32,128]{3,1,2,0:T(8,128)S(1)} fusion(f32[1,6,32,128]{3,1,2,0:T(8,128)S(1)} %fusion.283, f32[1,16,32,128]{3,1,2,0:T(8,128)S(1)} %get-tuple-element.6, f32[1,6,32,128]{3,1,2,0:T(8,128)S(1)} %fusion.282, f32[1,28,31,128]{3,1,2,0:T(8,128)S(1)} %get-tuple-element.57, f32[1,28,31,128]{3,1,2,0:T(8,128)S(1)} %get-tuple-element.56, ...), kind=kLoop, calls=%fused_computation.135 | loop fusion | flops 3784704 | bytes 6393856 | tf_op jit(solution)/shard_map/add | solution.py:68
  156.0 6.7 %all-to-all-done.3 = bf16[16,2,1,4096]{3,1,2,0:T(2,128)(2,1)} async-done(((bf16[16,2,1,4096]{3,1,2,0:T(2,128)(2,1)}), bf16[16,2,1,4096]{3,1,2,0:T(2,128)(2,1)}, u32[]{:S(2)}, u32[]{:S(2)}) %all-to-all-start.3) | async-done | bytes 262176 | tf_op jit(solution)/shard_map/all_to_all | solution.py:143
  162.7 1.0 reshape.2522
  163.7 1.4 gather_fusion.7
  166.8 2.7 %scatter_custom_fusion.3 = f32[512,128]{1,0:T(8,128)} fusion(s32[320]{0:T(512)} %copy-done.43, f32[320,128]{1,0:T(8,128)} %reshape.2426, f32[]{:T(128)} %constant.58.clone.1), kind=kCustom, calls=%fused_computation.501 | custom fusion | flops 40960 | bytes 262656 | tf_op jit(solution)/shard_map/scatter-add | solution.py:131
  169.5 3.9 %fusion.111 = f32[1,16,32,128]{3,1,2,0:T(8,128)S(1)} fusion(f32[1,16,32,128]{3,1,2,0:T(8,128)S(1)} %get-tuple-element.6, f32[1,6,32,128]{3,1,2,0:T(8,128)} %copy-done.6, f32[1,6,32,128]{3,1,2,0:T(8,128)S(1)} %fusion.283, f32[1,28,32,128]{3,1,2,0:T(8,128)S(1)} %fusion.16, f32[1,16,1,128]{3,1,2,0:T(8,128)} %get-tuple-element.127, ...), kind=kLoop, calls=%fused_computation.258 | loop fusion | flops 6946816 | bytes 8060928 | tf_op jit(solution)/shard_map/sub | solution.py:173
  181.6 2.0 collective-permute-start.5
  183.6 1.4 gather_fusion.10
  187.7 7.6 %all-to-all-start.4 = ((bf16[16,2,1,4096]{3,1,2,0:T(2,128)(2,1)}), bf16[16,2,1,4096]{3,1,2,0:T(2,128)(2,1)S(1)}, u32[]{:S(2)}, u32[]{:S(2)}) async-start(bf16[16,2,1,4096]{3,1,2,0:T(2,128)(2,1)} %reshape.2262), calls=%async_computation.4 | async-start | bytes 524288 | tf_op jit(solution)/shard_map/all_to_all | solution.py:154
  198.3 1.1 fusion.322
  200.4 1.0 fusion.318
  205.1 1.1 fusion.324
  206.2 1.4 fusion.42
  208.4 1.1 copy.218
  209.5 9.6 %all-to-all-start.5 = ((bf16[16,2,1,4096]{3,1,2,0:T(2,128)(2,1)}), bf16[16,2,1,4096]{3,1,2,0:T(2,128)(2,1)S(1)}, u32[]{:S(2)}, u32[]{:S(2)}) async-start(bf16[16,2,1,4096]{3,1,2,0:T(2,128)(2,1)} %bitcast.157), calls=%async_computation.5 | async-start | bytes 524288 | tf_op jit(solution)/shard_map/all_to_all | solution.py:143
  219.3 3.0 %fusion.7 = f32[1,28,32,128]{3,1,2,0:T(8,128)S(1)} fusion(f32[1,6,32,128]{3,1,2,0:T(8,128)S(1)} %fusion.281, f32[1,16,32,128]{3,1,2,0:T(8,128)S(1)} %fusion.111, f32[1,6,32,128]{3,1,2,0:T(8,128)S(1)} %fusion.280, f32[1,28,31,128]{3,1,2,0:T(8,128)S(1)} %get-tuple-element.35, f32[1,28,31,128]{3,1,2,0:T(8,128)S(1)} %get-tuple-element.34, ...), kind=kLoop, calls=%fused_computation.122 | loop fusion | flops 3784704 | bytes 6393856 | tf_op jit(solution)/shard_map/add | solution.py:68
  222.4 7.2 %all-to-all-done.5 = bf16[16,2,1,4096]{3,1,2,0:T(2,128)(2,1)S(1)} async-done(((bf16[16,2,1,4096]{3,1,2,0:T(2,128)(2,1)}), bf16[16,2,1,4096]{3,1,2,0:T(2,128)(2,1)S(1)}, u32[]{:S(2)}, u32[]{:S(2)}) %all-to-all-start.5) | async-done | bytes 262176 | tf_op jit(solution)/shard_map/all_to_all | solution.py:143
  231.3 1.8 scatter_custom_fusion.5
  233.2 3.4 %fusion.66 = f32[1,16,32,128]{3,1,2,0:T(8,128)S(1)} fusion(f32[1,16,32,128]{3,1,2,0:T(8,128)S(1)} %fusion.111, f32[1,6,32,128]{3,1,2,0:T(8,128)S(1)} %fusion.280, f32[1,6,32,128]{3,1,2,0:T(8,128)S(1)} %fusion.281, f32[1,28,32,128]{3,1,2,0:T(8,128)S(1)} %fusion.7, f32[1,16,1,128]{3,1,2,0:T(8,128)} %get-tuple-element.101, ...), kind=kLoop, calls=%fused_computation.213 | loop fusion | flops 7012352 | bytes 7798784 | tf_op jit(solution)/shard_map/sub | solution.py:174
  (245 shorter events, 63.4 us)
Async XLA Ops:
  6.5 6.9 %copy-start.51 = (s32[10]{0:T(128)S(1)}, s32[10]{0:T(128)}, u32[]{:S(2)}) copy-start(s32[10]{0:T(128)} %param.17) | copy-start | bytes 124
  6.5 23.6 %copy-start.52 = (s32[32]{0:T(128)S(1)}, s32[32]{0:T(128)}, u32[]{:S(2)}) copy-start(s32[32]{0:T(128)} %param.19) | copy-start | bytes 388
  7.7 50.7 %collective-permute-start = (f32[1,6,32,128]{3,1,2,0:T(8,128)S(1)}, f32[1,6,32,128]{3,1,2,0:T(8,128)S(1)}, u32[]{:S(2)}, u32[]{:S(2)}) collective-permute-start(f32[1,6,32,128]{3,1,2,0:T(8,128)S(1)} %get-tuple-element.157), channel_id=1, source_target_pairs={{16,0},{32,16},{48,32},{64,48},{80,64},{96,80},{112,96},{128,112},... | collective-permute-start | bytes 294920 | tf_op jit(solution)/shard_map/ppermute | solution.py:22
  9.6 49.4 %collective-permute-start.1 = (f32[1,6,32,128]{3,1,2,0:T(8,128)S(1)}, f32[1,6,32,128]{3,1,2,0:T(8,128)S(1)}, u32[]{:S(2)}, u32[]{:S(2)}) collective-permute-start(f32[1,6,32,128]{3,1,2,0:T(8,128)S(1)} %get-tuple-element.156), channel_id=1, source_target_pairs={{0,16},{16,32},{32,48},{48,64},{64,80},{80,96},{96,112},{112,128},... | collective-permute-start | bytes 294920 | tf_op jit(solution)/shard_map/ppermute | solution.py:21
  10.5 2.7 %copy-start.39 = (pred[10,32]{1,0:T(8,128)(4,1)}, pred[10,32]{1,0:T(8,128)(4,1)S(1)}, u32[]{:S(2)}) copy-start(pred[10,32]{1,0:T(8,128)(4,1)S(1)} %get-tuple-element.12) | copy-start | bytes 964
  13.4 22.9 %copy-start.53 = (bf16[1,2,8]{2,1,0:T(2,128)(2,1)S(1)}, bf16[1,2,8]{2,1,0:T(2,128)(2,1)}, u32[]{:S(2)}) copy-start(bf16[1,2,8]{2,1,0:T(2,128)(2,1)} %param.16) | copy-start | bytes 100
  14.2 41.7 %copy-start.50 = (s32[10]{0:T(128)}, s32[10]{0:T(128)S(1)}, u32[]{:S(2)}) copy-start(s32[10]{0:T(128)S(1)} %get-tuple-element.11) | copy-start | bytes 124
  15.9 50.8 %all-to-all-start = ((bf16[16,2,1,4096]{3,1,2,0:T(2,128)(2,1)}), bf16[16,2,1,4096]{3,1,2,0:T(2,128)(2,1)S(1)}, u32[]{:S(2)}, u32[]{:S(2)}) async-start(bf16[16,2,1,4096]{3,1,2,0:T(2,128)(2,1)} %reshape.2251), calls=%async_computation | async-start | bytes 524288 | tf_op jit(solution)/shard_map/all_to_all | solution.py:154
  29.4 40.2 %all-gather.2.cloned.1.call-start = ((), (), s32[]{:S(2)}) async-start(), calls=%async_computation.6 | async-start | bytes 2228224 | tf_op jit(solution)/shard_map/all_gather | solution.py:99
  30.2 29.4 %copy-start.48 = (pred[32]{0:T(512)(128)(4,1)}, pred[32]{0:T(512)(128)(4,1)S(1)}, u32[]{:S(2)}) copy-start(pred[32]{0:T(512)(128)(4,1)S(1)} %compare_and_fusion.3) | copy-start | bytes 100
  30.3 29.5 %copy-start.46 = (pred[32]{0:T(512)(128)(4,1)}, pred[32]{0:T(512)(128)(4,1)S(1)}, u32[]{:S(2)}) copy-start(pred[32]{0:T(512)(128)(4,1)S(1)} %compare_and_fusion.2) | copy-start | bytes 100
  36.2 22.8 %copy-start.44 = (s32[1024]{0:T(1024)}, s32[1024]{0:T(1024)S(1)}, u32[]{:S(2)}) copy-start(s32[1024]{0:T(1024)S(1)} %pad_clamp_fusion.3) | copy-start | bytes 12292
  59.9 24.6 %copy-start.5 = (f32[1,6,32,128]{3,1,2,0:T(8,128)}, f32[1,6,32,128]{3,1,2,0:T(8,128)S(1)}, u32[]{:S(2)}) copy-start(f32[1,6,32,128]{3,1,2,0:T(8,128)S(1)} %fusion.284) | copy-start | bytes 294916
  66.6 3.0 %copy-start.25 = (bf16[16,2,1,4096]{3,1,2,0:T(2,128)(2,1)}, bf16[16,2,1,4096]{3,1,2,0:T(2,128)(2,1)S(1)}, u32[]{:S(2)}) copy-start(bf16[16,2,1,4096]{3,1,2,0:T(2,128)(2,1)S(1)} %all-to-all-done) | copy-start | bytes 786436
  69.6 3.3 %copy-start = (bf16[1,32,8,4096]{3,2,0,1:T(8,128)(2,1)S(1)}, bf16[1,32,8,4096]{3,2,0,1:T(8,128)(2,1)}, u32[]{:S(2)}) copy-start(bf16[1,32,8,4096]{3,2,0,1:T(8,128)(2,1)} %all-gather.2.cloned.1.call-done) | copy-start | bytes 6291460
  74.7 21.7 %all-to-all-start.1 = ((bf16[16,2,1,4096]{3,1,2,0:T(2,128)(2,1)}), bf16[16,2,1,4096]{3,1,2,0:T(2,128)(2,1)}, u32[]{:S(2)}, u32[]{:S(2)}) async-start(bf16[16,2,1,4096]{3,1,2,0:T(2,128)(2,1)} %bitcast.153), calls=%async_computation.1 | async-start | bytes 524288 | tf_op jit(solution)/shard_map/all_to_all | solution.py:143
  88.2 15.0 %copy-start.2 = (f32[16,32,128]{2,1,0:T(8,128)S(1)}, f32[16,32,128]{2,1,0:T(8,128)}, u32[]{:S(2)}) copy-start(f32[16,32,128]{2,1,0:T(8,128)} %param.14) | copy-start | bytes 786436
  109.4 8.5 %copy-start.27 = (s32[1024]{0:T(1024)S(1)}, s32[1024]{0:T(1024)}, u32[]{:S(2)}) copy-start(s32[1024]{0:T(1024)} %copy-done.26) | copy-start | bytes 12292
  110.2 9.0 %copy-start.40 = (pred[10,32]{1,0:T(8,128)(4,1)S(1)}, pred[10,32]{1,0:T(8,128)(4,1)}, u32[]{:S(2)}) copy-start(pred[10,32]{1,0:T(8,128)(4,1)} %copy-done.39) | copy-start | bytes 964
  112.7 18.6 %copy-start.49 = (pred[32]{0:T(512)(128)(4,1)S(1)}, pred[32]{0:T(512)(128)(4,1)}, u32[]{:S(2)}) copy-start(pred[32]{0:T(512)(128)(4,1)} %copy-done.48) | copy-start | bytes 100
  112.7 18.7 %copy-start.47 = (pred[32]{0:T(512)(128)(4,1)S(1)}, pred[32]{0:T(512)(128)(4,1)}, u32[]{:S(2)}) copy-start(pred[32]{0:T(512)(128)(4,1)} %copy-done.46) | copy-start | bytes 100
  115.8 14.0 %collective-permute-start.2 = (f32[1,6,32,128]{3,1,2,0:T(8,128)S(1)}, f32[1,6,32,128]{3,1,2,0:T(8,128)S(1)}, u32[]{:S(2)}, u32[]{:S(2)}) collective-permute-start(f32[1,6,32,128]{3,1,2,0:T(8,128)S(1)} %get-tuple-element.130), channel_id=1, source_target_pairs={{16,0},{32,16},{48,32},{64,48},{80,64},{96,80},{112,96},{128,112},... | collective-permute-start | bytes 294920 | tf_op jit(solution)/shard_map/ppermute | solution.py:22
  115.9 14.6 %collective-permute-start.3 = (f32[1,6,32,128]{3,1,2,0:T(8,128)S(1)}, f32[1,6,32,128]{3,1,2,0:T(8,128)S(1)}, u32[]{:S(2)}, u32[]{:S(2)}) collective-permute-start(f32[1,6,32,128]{3,1,2,0:T(8,128)S(1)} %get-tuple-element.131), channel_id=1, source_target_pairs={{0,16},{16,32},{32,48},{48,64},{64,80},{80,96},{96,112},{112,128},... | collective-permute-start | bytes 294920 | tf_op jit(solution)/shard_map/ppermute | solution.py:21
  121.9 18.6 %all-to-all-start.2 = ((bf16[16,2,1,4096]{3,1,2,0:T(2,128)(2,1)}), bf16[16,2,1,4096]{3,1,2,0:T(2,128)(2,1)}, u32[]{:S(2)}, u32[]{:S(2)}) async-start(bf16[16,2,1,4096]{3,1,2,0:T(2,128)(2,1)} %reshape.2257), calls=%async_computation.2 | async-start | bytes 524288 | tf_op jit(solution)/shard_map/all_to_all | solution.py:154
  131.5 20.7 %copy-start.6 = (f32[1,6,32,128]{3,1,2,0:T(8,128)}, f32[1,6,32,128]{3,1,2,0:T(8,128)S(1)}, u32[]{:S(2)}) copy-start(f32[1,6,32,128]{3,1,2,0:T(8,128)S(1)} %fusion.282) | copy-start | bytes 294916
  144.7 18.0 %all-to-all-start.3 = ((bf16[16,2,1,4096]{3,1,2,0:T(2,128)(2,1)}), bf16[16,2,1,4096]{3,1,2,0:T(2,128)(2,1)}, u32[]{:S(2)}, u32[]{:S(2)}) async-start(bf16[16,2,1,4096]{3,1,2,0:T(2,128)(2,1)} %bitcast.155), calls=%async_computation.3 | async-start | bytes 524288 | tf_op jit(solution)/shard_map/all_to_all | solution.py:143
  156.0 13.5 %copy-start.1 = (f32[1,16,32,128]{3,2,1,0:T(8,128)S(1)}, f32[1,16,32,128]{3,2,1,0:T(8,128)}, u32[]{:S(2)}) copy-start(f32[1,16,32,128]{3,2,1,0:T(8,128)} %param.13) | copy-start | bytes 786436
  175.1 8.5 %copy-start.28 = (s32[1024]{0:T(1024)S(1)}, s32[1024]{0:T(1024)}, u32[]{:S(2)}) copy-start(s32[1024]{0:T(1024)} %copy-done.26) | copy-start | bytes 12292
  176.0 9.0 %copy-start.41 = (pred[10,32]{1,0:T(8,128)(4,1)S(1)}, pred[10,32]{1,0:T(8,128)(4,1)}, u32[]{:S(2)}) copy-start(pred[10,32]{1,0:T(8,128)(4,1)} %copy-done.39) | copy-start | bytes 964
  181.6 13.7 %collective-permute-start.4 = (f32[1,6,32,128]{3,1,2,0:T(8,128)S(1)}, f32[1,6,32,128]{3,1,2,0:T(8,128)S(1)}, u32[]{:S(2)}, u32[]{:S(2)}) collective-permute-start(f32[1,6,32,128]{3,1,2,0:T(8,128)S(1)} %get-tuple-element.104), channel_id=1, source_target_pairs={{16,0},{32,16},{48,32},{64,48},{80,64},{96,80},{112,96},{128,112},... | collective-permute-start | bytes 294920 | tf_op jit(solution)/shard_map/ppermute | solution.py:22
  181.6 14.4 %collective-permute-start.5 = (f32[1,6,32,128]{3,1,2,0:T(8,128)S(1)}, f32[1,6,32,128]{3,1,2,0:T(8,128)S(1)}, u32[]{:S(2)}, u32[]{:S(2)}) collective-permute-start(f32[1,6,32,128]{3,1,2,0:T(8,128)S(1)} %get-tuple-element.105), channel_id=1, source_target_pairs={{0,16},{16,32},{32,48},{48,64},{64,80},{80,96},{96,112},{112,128},... | collective-permute-start | bytes 294920 | tf_op jit(solution)/shard_map/ppermute | solution.py:21
  187.7 18.5 %all-to-all-start.4 = ((bf16[16,2,1,4096]{3,1,2,0:T(2,128)(2,1)}), bf16[16,2,1,4096]{3,1,2,0:T(2,128)(2,1)S(1)}, u32[]{:S(2)}, u32[]{:S(2)}) async-start(bf16[16,2,1,4096]{3,1,2,0:T(2,128)(2,1)} %reshape.2262), calls=%async_computation.4 | async-start | bytes 524288 | tf_op jit(solution)/shard_map/all_to_all | solution.py:154
  208.4 10.9 %copy-start.9 = (f32[1,28,30,128]{3,1,2,0:T(8,128)S(1)}, f32[1,28,30,128]{3,1,2,0:T(8,128)}, u32[]{:S(2)}) copy-start(f32[1,28,30,128]{3,1,2,0:T(8,128)} %get-tuple-element.32) | copy-start | bytes 1290244
  208.4 10.9 %copy-start.22 = (f32[1,28,4,128]{3,1,2,0:T(8,128)S(1)}, f32[1,28,4,128]{3,1,2,0:T(8,128)}, u32[]{:S(2)}) copy-start(f32[1,28,4,128]{3,1,2,0:T(8,128)} %get-tuple-element.22) | copy-start | bytes 172036
  208.4 10.9 %copy-start.33 = (f32[1,28,3,128]{3,1,2,0:T(8,128)S(1)}, f32[1,28,3,128]{3,1,2,0:T(8,128)}, u32[]{:S(2)}) copy-start(f32[1,28,3,128]{3,1,2,0:T(8,128)} %get-tuple-element.26) | copy-start | bytes 129028
  209.5 20.2 %all-to-all-start.5 = ((bf16[16,2,1,4096]{3,1,2,0:T(2,128)(2,1)}), bf16[16,2,1,4096]{3,1,2,0:T(2,128)(2,1)S(1)}, u32[]{:S(2)}, u32[]{:S(2)}) async-start(bf16[16,2,1,4096]{3,1,2,0:T(2,128)(2,1)} %bitcast.157), calls=%async_computation.5 | async-start | bytes 524288 | tf_op jit(solution)/shard_map/all_to_all | solution.py:143
  222.3 10.8 %copy-start.3 = (f32[16,32,128]{2,1,0:T(8,128)S(1)}, f32[16,32,128]{2,1,0:T(8,128)}, u32[]{:S(2)}) copy-start(f32[16,32,128]{2,1,0:T(8,128)} %param.14) | copy-start | bytes 786436
  222.3 10.8 %copy-start.4 = (f32[1,16,32,128]{3,1,2,0:T(8,128)S(1)}, f32[1,16,32,128]{3,1,2,0:T(8,128)}, u32[]{:S(2)}) copy-start(f32[1,16,32,128]{3,1,2,0:T(8,128)} %get-tuple-element.8) | copy-start | bytes 786436
  222.3 10.8 %copy-start.16 = (f32[1,16,31,128]{3,1,2,0:T(8,128)S(1)}, f32[1,16,31,128]{3,1,2,0:T(8,128)}, u32[]{:S(2)}) copy-start(f32[1,16,31,128]{3,1,2,0:T(8,128)} %get-tuple-element.102) | copy-start | bytes 761860
  222.4 10.8 %copy-start.17 = (f32[1,16,31,128]{3,1,2,0:T(8,128)S(1)}, f32[1,16,31,128]{3,1,2,0:T(8,128)}, u32[]{:S(2)}) copy-start(f32[1,16,31,128]{3,1,2,0:T(8,128)} %get-tuple-element.103) | copy-start | bytes 761860
  222.4 10.8 %copy-start.18 = (f32[1,16,30,128]{3,1,2,0:T(8,128)S(1)}, f32[1,16,30,128]{3,1,2,0:T(8,128)}, u32[]{:S(2)}) copy-start(f32[1,16,30,128]{3,1,2,0:T(8,128)} %get-tuple-element.98) | copy-start | bytes 737284
  222.4 10.8 %copy-start.19 = (f32[1,16,30,128]{3,1,2,0:T(8,128)S(1)}, f32[1,16,30,128]{3,1,2,0:T(8,128)}, u32[]{:S(2)}) copy-start(f32[1,16,30,128]{3,1,2,0:T(8,128)} %get-tuple-element.99) | copy-start | bytes 737284
  222.4 10.8 %copy-start.29 = (f32[1,16,6,128]{3,1,2,0:T(8,128)S(1)}, f32[1,16,6,128]{3,1,2,0:T(8,128)}, u32[]{:S(2)}) copy-start(f32[1,16,6,128]{3,1,2,0:T(8,128)} %get-tuple-element.80) | copy-start | bytes 147460
  222.4 10.8 %copy-start.30 = (f32[1,16,6,128]{3,1,2,0:T(8,128)S(1)}, f32[1,16,6,128]{3,1,2,0:T(8,128)}, u32[]{:S(2)}) copy-start(f32[1,16,6,128]{3,1,2,0:T(8,128)} %get-tuple-element.81) | copy-start | bytes 147460
  222.4 10.8 %copy-start.36 = (f32[1,16,5,128]{3,1,2,0:T(8,128)S(1)}, f32[1,16,5,128]{3,1,2,0:T(8,128)}, u32[]{:S(2)}) copy-start(f32[1,16,5,128]{3,1,2,0:T(8,128)} %get-tuple-element.84) | copy-start | bytes 122884
  222.4 10.8 %copy-start.37 = (f32[1,16,4,128]{3,1,2,0:T(8,128)S(1)}, f32[1,16,4,128]{3,1,2,0:T(8,128)}, u32[]{:S(2)}) copy-start(f32[1,16,4,128]{3,1,2,0:T(8,128)} %get-tuple-element.88) | copy-start | bytes 98308
  222.4 10.8 %copy-start.38 = (f32[1,16,2,128]{3,1,2,0:T(8,128)S(1)}, f32[1,16,2,128]{3,1,2,0:T(8,128)}, u32[]{:S(2)}) copy-start(f32[1,16,2,128]{3,1,2,0:T(8,128)} %get-tuple-element.96) | copy-start | bytes 49156
  222.4 10.8 %copy-start.42 = (f32[1,16,1,128]{3,1,2,0:T(8,128)S(1)}, f32[1,16,1,128]{3,1,2,0:T(8,128)}, u32[]{:S(2)}) copy-start(f32[1,16,1,128]{3,1,2,0:T(8,128)} %get-tuple-element.100) | copy-start | bytes 24580
  (19 other events, 25.3 us)
Sparse Core Ops, SparseCore 0:
  32.0 37.4 all-gather.1
where the time goes:
time: 245 us; the launch traced here: 244 us
  local copies, waits for them, and re-layouts  77.8 us (32%)
  starting transfers between devices  61.8 us (25%)
  other arithmetic  34.1 us (14%)
  waiting for transfers between devices  28.1 us (11%)
  blocking collectives  18.8 us (8%)
  between operations  14.5 us (6%)
  matrix products  9.17 us (4%)
    all_to_all x3, starting transfers between devices, nonlocal_part(): lax.all_to_all(outbox, 'grid', split_axis=0, concat_axis=0, tiled=True)  29.1 us
    all_to_all x3, starting transfers between devices, at_owner(): lax.all_to_all(projected, 'grid', split_axis=0, concat_axis=0, tiled=True)  26.5 us
    all_to_all x3, waiting for transfers between devices, at_owner(): lax.all_to_all(projected, 'grid', split_axis=0, concat_axis=0, tiled=True)  22.1 us
    slice x33, local copies, waits for them, and re-layouts, laplacian(): jnp.roll(padded, k, 2)  21.4 us
    all_gather x1, blocking collectives, shards(): lax.all_gather(proj_gains, 'states', axis=1, tiled=True)  18.8 us
    slice x24, local copies, waits for them, and re-layouts, laplacian(): jnp.roll(interior, k, 2)  17.4 us
    slice x12, local copies, waits for them, and re-layouts, laplacian(): jnp.roll(interior, -k, 2) + jnp.roll(interior, k, 2)  8.69 us
    add x3, other arithmetic, laplacian(): y_slope + first_weights[k] * (jnp.roll(padded, -k, 2) - jnp.roll(padded,...  7.96 us
  transfers between devices with their start and end apart: 13, of which 5 were waited for; matrix products, arithmetic and copies ran while one was open for 24% of the time, Pallas kernels for 0%

commit v1 on v0

--- a/solution.py
+++ b/solution.py
@@ -97,7 +97,10 @@
     local_rows = jnp.where(atom_rows >= 0, atom_rows - tile_index * tile_lines, tile_lines)
     full_proj, full_gain = (
         lax.all_gather(projectors, "states", axis=1, tiled=True),
-        lax.all_gather(proj_gains, "states", axis=1, tiled=True),
+        jnp.concatenate(
+            lax.all_to_all(jnp.stack([proj_gains] * lax.axis_size("states")), "states", 0, 0),
+            axis=1,
+        ),
     )
     full_proj = full_proj.reshape(n_grid, PAIR_CAP, proj_count, line_span)
     full_gain = full_gain.reshape(n_grid, PAIR_CAP, proj_count)

time: 245 us -> 244 us (level)
  blocking collectives: 18.8 us -> 0 us
  waiting for transfers between devices: 28.1 us -> 42.7 us
  starting transfers between devices: 61.8 us -> 65.5 us
    all_gather x1 -> x0, blocking collectives: 18.8 us -> none  [shards(): lax.all_gather(proj_gains, 'states', axis=1, tiled=True)]
    all_gather x1, waiting for transfers between devices: 2.95 us -> 16.7 us  [shards(): lax.all_gather(projectors, 'states', axis=1, tiled=True)]
    all_to_all x0 -> x1, starting transfers between devices: none -> 4.52 us  [shards(): lax.all_to_all(jnp.stack([proj_gains] * lax.axis_size('states')), 'states...]
  transfers between devices with their start and end apart: 13 -> 14, of which waited for: 5 -> 6; matrix products, arithmetic and copies ran while one was open for 24% -> 25% of each run, Pallas kernels for 0% -> 0%
where the time goes in v1:
time: 244 us; the launch traced here: 243 us
  local copies, waits for them, and re-layouts  77.9 us (32%)
  starting transfers between devices  65.5 us (27%)
  waiting for transfers between devices  42.7 us (18%)
  other arithmetic  32.8 us (13%)
  between operations  14.5 us (6%)
  matrix products  9.17 us (4%)
    all_to_all x3, starting transfers between devices, nonlocal_part(): lax.all_to_all(outbox, 'grid', split_axis=0, concat_axis=0, tiled=True)  29.1 us
    all_to_all x3, starting transfers between devices, at_owner(): lax.all_to_all(projected, 'grid', split_axis=0, concat_axis=0, tiled=True)  25.8 us
    all_to_all x3, waiting for transfers between devices, at_owner(): lax.all_to_all(projected, 'grid', split_axis=0, concat_axis=0, tiled=True)  22.1 us
    slice x33, local copies, waits for them, and re-layouts, laplacian(): jnp.roll(padded, k, 2)  21.4 us
    slice x24, local copies, waits for them, and re-layouts, laplacian(): jnp.roll(interior, k, 2)  17.4 us
    all_gather x1, waiting for transfers between devices, shards(): lax.all_gather(projectors, 'states', axis=1, tiled=True)  16.7 us
    slice x12, local copies, waits for them, and re-layouts, laplacian(): jnp.roll(interior, -k, 2) + jnp.roll(interior, k, 2)  8.69 us
    add x3, other arithmetic, laplacian(): y_slope + first_weights[k] * (jnp.roll(padded, -k, 2) - jnp.roll(padded,...  7.96 us
  transfers between devices with their start and end apart: 14, of which 6 were waited for; matrix products, arithmetic and copies ran while one was open for 25% of the time, Pallas kernels for 0%

profile of v1, /device:TPU:32, one launch (start us, length us, event | category | flops | bytes accessed | tf_op | source)
XLA Modules:
  0.0 242.6 jit_solution(5326627559402964139)
XLA Ops:
  6.5 1.1 copy.127
  7.7 1.9 collective-permute-start
  10.6 2.1 gather_fusion.2
  15.3 13.5 %all-to-all-start = ((bf16[16,2,1,4096]{3,1,2,0:T(2,128)(2,1)}), bf16[16,2,1,4096]{3,1,2,0:T(2,128)(2,1)S(1)}, u32[]{:S(2)}, u32[]{:S(2)}) async-start(bf16[16,2,1,4096]{3,1,2,0:T(2,128)(2,1)} %reshape.2254), calls=%async_computation | async-start | bytes 524288 | tf_op jit(solution)/shard_map/all_to_all | solution.py:157
  41.9 1.1 fusion.341
  45.0 1.1 fusion.347
  46.1 1.1 fusion.349
  47.8 4.5 %all-to-all-start.1 = ((bf16[16,1,2,8]{3,2,1,0:T(2,128)(2,1)}), bf16[16,1,2,8]{3,2,1,0:T(2,128)(2,1)S(1)}, u32[]{:S(2)}, u32[]{:S(2)}) async-start(bf16[16,1,2,8]{3,2,1,0:T(2,128)(2,1)} %stack.2), calls=%async_computation.1 | async-start | bytes 16384 | tf_op jit(solution)/shard_map/all_to_all | solution.py:101
  52.4 16.7 %all-gather.2.cloned.1.call-done = bf16[1,32,8,4096]{3,2,0,1:T(8,128)(2,1)} async-done(((bf16[1,2,8,4096]{3,2,0,1:T(8,128)(2,1)}), bf16[1,32,8,4096]{3,2,0,1:T(8,128)(2,1)}) %all-gather.2.cloned.1.call-update) | async-done | bytes 2097168 | tf_op jit(solution)/shard_map/all_gather | solution.py:99
  69.0 3.3 %fusion.46 = f32[16,2,1,8]{3,2,1,0:T(1,128)S(1)} fusion(bf16[16,2,8,4096]{3,2,1,0:T(8,128)(2,1)} %bitcast.163, bf16[16,2,4096,1]{2,1,0,3:T(2,128)(2,1)} %bitcast.187), kind=kOutput, calls=%fused_computation.193 | convolution fusion | flops 2097152 | bytes 2360320 | tf_op jit(solution)/shard_map/gpjc,gpsc->gpsj/dot_general | solution.py:139
  73.0 1.1 copy.214
  74.2 9.7 %all-to-all-start.2 = ((bf16[16,2,1,4096]{3,1,2,0:T(2,128)(2,1)}), bf16[16,2,1,4096]{3,1,2,0:T(2,128)(2,1)}, u32[]{:S(2)}, u32[]{:S(2)}) async-start(bf16[16,2,1,4096]{3,1,2,0:T(2,128)(2,1)} %bitcast.158), calls=%async_computation.2 | async-start | bytes 524288 | tf_op jit(solution)/shard_map/all_to_all | solution.py:146
  85.4 2.5 %fusion.25 = f32[1,28,32,128]{3,1,2,0:T(8,128)S(1)} fusion(f32[1,6,32,128]{3,1,2,0:T(8,128)S(1)} %fusion.285, f32[1,16,32,128]{3,1,2,0:T(8,128)S(1)} %copy.127, f32[1,6,32,128]{3,1,2,0:T(8,128)S(1)} %fusion.284, f32[1,28,31,128]{3,1,2,0:T(8,128)S(1)} %get-tuple-element.79, f32[1,28,31,128]{3,1,2,0:T(8,128)S(1)} %get-tuple-element.78, ...), kind=kLoop, calls=%fused_computation.148 | loop fusion | flops 3784704 | bytes 6393856 | tf_op jit(solution)/shard_map/add | solution.py:68
  87.9 8.2 %all-to-all-done.2 = bf16[16,2,1,4096]{3,1,2,0:T(2,128)(2,1)} async-done(((bf16[16,2,1,4096]{3,1,2,0:T(2,128)(2,1)}), bf16[16,2,1,4096]{3,1,2,0:T(2,128)(2,1)}, u32[]{:S(2)}, u32[]{:S(2)}) %all-to-all-start.2) | async-done | bytes 262176 | tf_op jit(solution)/shard_map/all_to_all | solution.py:146
  96.0 1.0 reshape.2508
  97.1 1.4 gather_fusion.3
  100.2 2.7 %scatter_custom_fusion.1 = f32[512,128]{1,0:T(8,128)} fusion(s32[320]{0:T(512)} %copy-done.39, f32[320,128]{1,0:T(8,128)} %reshape.2409, f32[]{:T(128)} %constant.58.clone.1), kind=kCustom, calls=%fused_computation.503 | custom fusion | flops 40960 | bytes 262656 | tf_op jit(solution)/shard_map/scatter-add | solution.py:134
  102.9 4.3 %broadcast_multiply_fusion = (f32[1,16,32,128]{3,1,2,0:T(8,128)S(1)}, f32[1,16,32,128]{3,1,2,0:T(8,128)}) fusion(f32[1,16,32,128]{3,1,2,0:T(8,128)S(1)} %copy.127, f32[1,16,32,128]{3,2,1,0:T(8,128)} %bitcast.173, f32[16,32,128]{2,1,0:T(8,128)S(1)} %copy-done.2, f32[1,28,32,128]{3,1,2,0:T(8,128)S(1)} %fusion.25, f32[1,16,26,128]{3,1,2,0:T(8,128)} %get-tuple-element.153, ...), kind=kLoop, calls=%fused_computation.505 | loop fusion | flops 6881280 | bytes 7798784 | tf_op jit(solution)/shard_map/div | solution.py:173
  115.5 1.9 collective-permute-start.3
  117.5 1.4 gather_fusion.6
  121.5 7.9 %all-to-all-start.3 = ((bf16[16,2,1,4096]{3,1,2,0:T(2,128)(2,1)}), bf16[16,2,1,4096]{3,1,2,0:T(2,128)(2,1)}, u32[]{:S(2)}, u32[]{:S(2)}) async-start(bf16[16,2,1,4096]{3,1,2,0:T(2,128)(2,1)} %reshape.2260), calls=%async_computation.3 | async-start | bytes 524288 | tf_op jit(solution)/shard_map/all_to_all | solution.py:157
  131.2 1.1 fusion.336
  133.3 1.0 fusion.332
  136.7 1.1 fusion.338
  137.8 2.3 all-to-all-done.3
  140.1 2.4 fusion.44
  143.2 1.1 copy.215
  144.3 7.3 %all-to-all-start.4 = ((bf16[16,2,1,4096]{3,1,2,0:T(2,128)(2,1)}), bf16[16,2,1,4096]{3,1,2,0:T(2,128)(2,1)}, u32[]{:S(2)}, u32[]{:S(2)}) async-start(bf16[16,2,1,4096]{3,1,2,0:T(2,128)(2,1)} %bitcast.160), calls=%async_computation.4 | async-start | bytes 524288 | tf_op jit(solution)/shard_map/all_to_all | solution.py:146
  153.1 2.5 %fusion.16 = f32[1,28,32,128]{3,1,2,0:T(8,128)S(1)} fusion(f32[1,6,32,128]{3,1,2,0:T(8,128)S(1)} %fusion.283, f32[1,16,32,128]{3,1,2,0:T(8,128)S(1)} %get-tuple-element.6, f32[1,6,32,128]{3,1,2,0:T(8,128)S(1)} %fusion.282, f32[1,28,31,128]{3,1,2,0:T(8,128)S(1)} %get-tuple-element.57, f32[1,28,31,128]{3,1,2,0:T(8,128)S(1)} %get-tuple-element.56, ...), kind=kLoop, calls=%fused_computation.135 | loop fusion | flops 3784704 | bytes 6393856 | tf_op jit(solution)/shard_map/add | solution.py:68
  155.6 6.7 %all-to-all-done.4 = bf16[16,2,1,4096]{3,1,2,0:T(2,128)(2,1)} async-done(((bf16[16,2,1,4096]{3,1,2,0:T(2,128)(2,1)}), bf16[16,2,1,4096]{3,1,2,0:T(2,128)(2,1)}, u32[]{:S(2)}, u32[]{:S(2)}) %all-to-all-start.4) | async-done | bytes 262176 | tf_op jit(solution)/shard_map/all_to_all | solution.py:146
  162.3 1.0 reshape.2525
  163.3 1.4 gather_fusion.7
  166.4 2.7 %scatter_custom_fusion.3 = f32[512,128]{1,0:T(8,128)} fusion(s32[320]{0:T(512)} %copy-done.39, f32[320,128]{1,0:T(8,128)} %reshape.2429, f32[]{:T(128)} %constant.58.clone.1), kind=kCustom, calls=%fused_computation.501 | custom fusion | flops 40960 | bytes 262656 | tf_op jit(solution)/shard_map/scatter-add | solution.py:134
  169.1 3.9 %fusion.111 = f32[1,16,32,128]{3,1,2,0:T(8,128)S(1)} fusion(f32[1,16,32,128]{3,1,2,0:T(8,128)S(1)} %get-tuple-element.6, f32[1,6,32,128]{3,1,2,0:T(8,128)} %copy-done.6, f32[1,6,32,128]{3,1,2,0:T(8,128)S(1)} %fusion.283, f32[1,28,32,128]{3,1,2,0:T(8,128)S(1)} %fusion.16, f32[1,16,1,128]{3,1,2,0:T(8,128)} %get-tuple-element.127, ...), kind=kLoop, calls=%fused_computation.258 | loop fusion | flops 6946816 | bytes 8060928 | tf_op jit(solution)/shard_map/sub | solution.py:176
  181.2 2.0 collective-permute-start.5
  183.3 1.4 gather_fusion.10
  187.3 7.6 %all-to-all-start.5 = ((bf16[16,2,1,4096]{3,1,2,0:T(2,128)(2,1)}), bf16[16,2,1,4096]{3,1,2,0:T(2,128)(2,1)S(1)}, u32[]{:S(2)}, u32[]{:S(2)}) async-start(bf16[16,2,1,4096]{3,1,2,0:T(2,128)(2,1)} %reshape.2265), calls=%async_computation.5 | async-start | bytes 524288 | tf_op jit(solution)/shard_map/all_to_all | solution.py:157
  196.7 1.1 fusion.325
  197.7 1.0 fusion.323
  198.8 1.0 fusion.321
  203.4 1.1 fusion.327
  205.5 1.4 fusion.42
  207.7 1.1 copy.216
  208.8 8.7 %all-to-all-start.6 = ((bf16[16,2,1,4096]{3,1,2,0:T(2,128)(2,1)}), bf16[16,2,1,4096]{3,1,2,0:T(2,128)(2,1)S(1)}, u32[]{:S(2)}, u32[]{:S(2)}) async-start(bf16[16,2,1,4096]{3,1,2,0:T(2,128)(2,1)} %bitcast.162), calls=%async_computation.6 | async-start | bytes 524288 | tf_op jit(solution)/shard_map/all_to_all | solution.py:146
  217.6 3.0 %fusion.7 = f32[1,28,32,128]{3,1,2,0:T(8,128)S(1)} fusion(f32[1,6,32,128]{3,1,2,0:T(8,128)S(1)} %fusion.281, f32[1,16,32,128]{3,1,2,0:T(8,128)S(1)} %fusion.111, f32[1,6,32,128]{3,1,2,0:T(8,128)S(1)} %fusion.280, f32[1,28,31,128]{3,1,2,0:T(8,128)S(1)} %get-tuple-element.35, f32[1,28,31,128]{3,1,2,0:T(8,128)S(1)} %get-tuple-element.34, ...), kind=kLoop, calls=%fused_computation.122 | loop fusion | flops 3784704 | bytes 6393856 | tf_op jit(solution)/shard_map/add | solution.py:68
  220.8 7.3 %all-to-all-done.6 = bf16[16,2,1,4096]{3,1,2,0:T(2,128)(2,1)S(1)} async-done(((bf16[16,2,1,4096]{3,1,2,0:T(2,128)(2,1)}), bf16[16,2,1,4096]{3,1,2,0:T(2,128)(2,1)S(1)}, u32[]{:S(2)}, u32[]{:S(2)}) %all-to-all-start.6) | async-done | bytes 262176 | tf_op jit(solution)/shard_map/all_to_all | solution.py:146
  229.6 1.8 scatter_custom_fusion.5
  231.5 3.4 %fusion.66 = f32[1,16,32,128]{3,1,2,0:T(8,128)S(1)} fusion(f32[1,16,32,128]{3,1,2,0:T(8,128)S(1)} %fusion.111, f32[1,6,32,128]{3,1,2,0:T(8,128)S(1)} %fusion.280, f32[1,6,32,128]{3,1,2,0:T(8,128)S(1)} %fusion.281, f32[1,28,32,128]{3,1,2,0:T(8,128)S(1)} %fusion.7, f32[1,16,1,128]{3,1,2,0:T(8,128)} %get-tuple-element.101, ...), kind=kLoop, calls=%fused_computation.213 | loop fusion | flops 7012352 | bytes 7798784 | tf_op jit(solution)/shard_map/sub | solution.py:177
  (241 shorter events, 63.1 us)
Async XLA Ops:
  6.5 6.3 %copy-start.50 = (s32[10]{0:T(128)S(1)}, s32[10]{0:T(128)}, u32[]{:S(2)}) copy-start(s32[10]{0:T(128)} %param.17) | copy-start | bytes 124
  6.5 23.0 %copy-start.51 = (s32[32]{0:T(128)S(1)}, s32[32]{0:T(128)}, u32[]{:S(2)}) copy-start(s32[32]{0:T(128)} %param.19) | copy-start | bytes 388
  7.7 31.3 %collective-permute-start = (f32[1,6,32,128]{3,1,2,0:T(8,128)S(1)}, f32[1,6,32,128]{3,1,2,0:T(8,128)S(1)}, u32[]{:S(2)}, u32[]{:S(2)}) collective-permute-start(f32[1,6,32,128]{3,1,2,0:T(8,128)S(1)} %get-tuple-element.157), channel_id=1, source_target_pairs={{16,0},{32,16},{48,32},{64,48},{80,64},{96,80},{112,96},{128,112},... | collective-permute-start | bytes 294920 | tf_op jit(solution)/shard_map/ppermute | solution.py:22
  9.6 30.0 %collective-permute-start.1 = (f32[1,6,32,128]{3,1,2,0:T(8,128)S(1)}, f32[1,6,32,128]{3,1,2,0:T(8,128)S(1)}, u32[]{:S(2)}, u32[]{:S(2)}) collective-permute-start(f32[1,6,32,128]{3,1,2,0:T(8,128)S(1)} %get-tuple-element.156), channel_id=1, source_target_pairs={{0,16},{16,32},{32,48},{48,64},{64,80},{80,96},{96,112},{112,128},... | collective-permute-start | bytes 294920 | tf_op jit(solution)/shard_map/ppermute | solution.py:21
  10.6 21.3 %copy-start.39 = (s32[320]{0:T(512)}, s32[320]{0:T(512)S(1)}, u32[]{:S(2)}) copy-start(s32[320]{0:T(512)S(1)} %reshape.2407) | copy-start | bytes 3844
  13.6 22.9 %copy-start.48 = (s32[10]{0:T(128)}, s32[10]{0:T(128)S(1)}, u32[]{:S(2)}) copy-start(s32[10]{0:T(128)S(1)} %get-tuple-element.11) | copy-start | bytes 124
  15.3 31.9 %all-to-all-start = ((bf16[16,2,1,4096]{3,1,2,0:T(2,128)(2,1)}), bf16[16,2,1,4096]{3,1,2,0:T(2,128)(2,1)S(1)}, u32[]{:S(2)}, u32[]{:S(2)}) async-start(bf16[16,2,1,4096]{3,1,2,0:T(2,128)(2,1)} %reshape.2254), calls=%async_computation | async-start | bytes 524288 | tf_op jit(solution)/shard_map/all_to_all | solution.py:157
  28.8 40.3 %all-gather.2.cloned.1.call-start = ((), (), s32[]{:S(2)}) async-start(), calls=%async_computation.7 | async-start | bytes 2228224 | tf_op jit(solution)/shard_map/all_gather | solution.py:99
  29.6 10.6 %copy-start.45 = (pred[32]{0:T(512)(128)(4,1)}, pred[32]{0:T(512)(128)(4,1)S(1)}, u32[]{:S(2)}) copy-start(pred[32]{0:T(512)(128)(4,1)S(1)} %compare_and_fusion.3) | copy-start | bytes 100
  29.7 10.7 %copy-start.42 = (pred[32]{0:T(512)(128)(4,1)}, pred[32]{0:T(512)(128)(4,1)S(1)}, u32[]{:S(2)}) copy-start(pred[32]{0:T(512)(128)(4,1)S(1)} %compare_and_fusion.2) | copy-start | bytes 100
  35.6 4.6 %copy-start.40 = (s32[1024]{0:T(1024)}, s32[1024]{0:T(1024)S(1)}, u32[]{:S(2)}) copy-start(s32[1024]{0:T(1024)S(1)} %pad_clamp_fusion.3) | copy-start | bytes 12292
  39.0 4.0 %copy-start.41 = (s32[1024]{0:T(1024)}, s32[1024]{0:T(1024)S(1)}, u32[]{:S(2)}) copy-start(s32[1024]{0:T(1024)S(1)} %pad_clamp_fusion.2) | copy-start | bytes 12292
  40.5 43.6 %copy-start.5 = (f32[1,6,32,128]{3,1,2,0:T(8,128)}, f32[1,6,32,128]{3,1,2,0:T(8,128)S(1)}, u32[]{:S(2)}) copy-start(f32[1,6,32,128]{3,1,2,0:T(8,128)S(1)} %fusion.284) | copy-start | bytes 294916
  47.2 21.9 %copy-start.25 = (bf16[16,2,1,4096]{3,1,2,0:T(2,128)(2,1)}, bf16[16,2,1,4096]{3,1,2,0:T(2,128)(2,1)S(1)}, u32[]{:S(2)}) copy-start(bf16[16,2,1,4096]{3,1,2,0:T(2,128)(2,1)S(1)} %all-to-all-done) | copy-start | bytes 786436
  47.8 24.5 %all-to-all-start.1 = ((bf16[16,1,2,8]{3,2,1,0:T(2,128)(2,1)}), bf16[16,1,2,8]{3,2,1,0:T(2,128)(2,1)S(1)}, u32[]{:S(2)}, u32[]{:S(2)}) async-start(bf16[16,1,2,8]{3,2,1,0:T(2,128)(2,1)} %stack.2), calls=%async_computation.1 | async-start | bytes 16384 | tf_op jit(solution)/shard_map/all_to_all | solution.py:101
  69.0 3.3 %copy-start = (bf16[1,32,8,4096]{3,2,0,1:T(8,128)(2,1)S(1)}, bf16[1,32,8,4096]{3,2,0,1:T(8,128)(2,1)}, u32[]{:S(2)}) copy-start(bf16[1,32,8,4096]{3,2,0,1:T(8,128)(2,1)} %all-gather.2.cloned.1.call-done) | copy-start | bytes 6291460
  72.3 70.2 %copy-start.34 = (bf16[16,1,2,8]{3,2,1,0:T(2,128)(2,1)}, bf16[16,1,2,8]{3,2,1,0:T(2,128)(2,1)S(1)}, u32[]{:S(2)}) copy-start(bf16[16,1,2,8]{3,2,1,0:T(2,128)(2,1)S(1)} %all-to-all-done.1) | copy-start | bytes 1540
  74.2 21.9 %all-to-all-start.2 = ((bf16[16,2,1,4096]{3,1,2,0:T(2,128)(2,1)}), bf16[16,2,1,4096]{3,1,2,0:T(2,128)(2,1)}, u32[]{:S(2)}, u32[]{:S(2)}) async-start(bf16[16,2,1,4096]{3,1,2,0:T(2,128)(2,1)} %bitcast.158), calls=%async_computation.2 | async-start | bytes 524288 | tf_op jit(solution)/shard_map/all_to_all | solution.py:146
  87.9 15.0 %copy-start.2 = (f32[16,32,128]{2,1,0:T(8,128)S(1)}, f32[16,32,128]{2,1,0:T(8,128)}, u32[]{:S(2)}) copy-start(f32[16,32,128]{2,1,0:T(8,128)} %param.14) | copy-start | bytes 786436
  112.3 18.6 %copy-start.46 = (pred[32]{0:T(512)(128)(4,1)S(1)}, pred[32]{0:T(512)(128)(4,1)}, u32[]{:S(2)}) copy-start(pred[32]{0:T(512)(128)(4,1)} %copy-done.45) | copy-start | bytes 100
  112.3 18.7 %copy-start.43 = (pred[32]{0:T(512)(128)(4,1)S(1)}, pred[32]{0:T(512)(128)(4,1)}, u32[]{:S(2)}) copy-start(pred[32]{0:T(512)(128)(4,1)} %copy-done.42) | copy-start | bytes 100
  115.4 14.0 %collective-permute-start.2 = (f32[1,6,32,128]{3,1,2,0:T(8,128)S(1)}, f32[1,6,32,128]{3,1,2,0:T(8,128)S(1)}, u32[]{:S(2)}, u32[]{:S(2)}) collective-permute-start(f32[1,6,32,128]{3,1,2,0:T(8,128)S(1)} %get-tuple-element.130), channel_id=1, source_target_pairs={{16,0},{32,16},{48,32},{64,48},{80,64},{96,80},{112,96},{128,112},... | collective-permute-start | bytes 294920 | tf_op jit(solution)/shard_map/ppermute | solution.py:22
  115.5 14.6 %collective-permute-start.3 = (f32[1,6,32,128]{3,1,2,0:T(8,128)S(1)}, f32[1,6,32,128]{3,1,2,0:T(8,128)S(1)}, u32[]{:S(2)}, u32[]{:S(2)}) collective-permute-start(f32[1,6,32,128]{3,1,2,0:T(8,128)S(1)} %get-tuple-element.131), channel_id=1, source_target_pairs={{0,16},{16,32},{32,48},{48,64},{64,80},{80,96},{96,112},{112,128},... | collective-permute-start | bytes 294920 | tf_op jit(solution)/shard_map/ppermute | solution.py:21
  121.5 18.6 %all-to-all-start.3 = ((bf16[16,2,1,4096]{3,1,2,0:T(2,128)(2,1)}), bf16[16,2,1,4096]{3,1,2,0:T(2,128)(2,1)}, u32[]{:S(2)}, u32[]{:S(2)}) async-start(bf16[16,2,1,4096]{3,1,2,0:T(2,128)(2,1)} %reshape.2260), calls=%async_computation.3 | async-start | bytes 524288 | tf_op jit(solution)/shard_map/all_to_all | solution.py:157
  131.1 20.7 %copy-start.6 = (f32[1,6,32,128]{3,1,2,0:T(8,128)}, f32[1,6,32,128]{3,1,2,0:T(8,128)S(1)}, u32[]{:S(2)}) copy-start(f32[1,6,32,128]{3,1,2,0:T(8,128)S(1)} %fusion.282) | copy-start | bytes 294916
  144.3 18.0 %all-to-all-start.4 = ((bf16[16,2,1,4096]{3,1,2,0:T(2,128)(2,1)}), bf16[16,2,1,4096]{3,1,2,0:T(2,128)(2,1)}, u32[]{:S(2)}, u32[]{:S(2)}) async-start(bf16[16,2,1,4096]{3,1,2,0:T(2,128)(2,1)} %bitcast.160), calls=%async_computation.4 | async-start | bytes 524288 | tf_op jit(solution)/shard_map/all_to_all | solution.py:146
  155.6 13.5 %copy-start.1 = (f32[1,16,32,128]{3,2,1,0:T(8,128)S(1)}, f32[1,16,32,128]{3,2,1,0:T(8,128)}, u32[]{:S(2)}) copy-start(f32[1,16,32,128]{3,2,1,0:T(8,128)} %param.13) | copy-start | bytes 786436
  155.6 13.5 %copy-start.38 = (f32[1,16,1,128]{3,1,2,0:T(8,128)S(1)}, f32[1,16,1,128]{3,1,2,0:T(8,128)}, u32[]{:S(2)}) copy-start(f32[1,16,1,128]{3,1,2,0:T(8,128)} %get-tuple-element.126) | copy-start | bytes 24580
  178.1 18.3 %copy-start.47 = (pred[32]{0:T(512)(128)(4,1)S(1)}, pred[32]{0:T(512)(128)(4,1)}, u32[]{:S(2)}) copy-start(pred[32]{0:T(512)(128)(4,1)} %copy-done.45) | copy-start | bytes 100
  178.1 18.4 %copy-start.44 = (pred[32]{0:T(512)(128)(4,1)S(1)}, pred[32]{0:T(512)(128)(4,1)}, u32[]{:S(2)}) copy-start(pred[32]{0:T(512)(128)(4,1)} %copy-done.42) | copy-start | bytes 100
  181.2 13.7 %collective-permute-start.4 = (f32[1,6,32,128]{3,1,2,0:T(8,128)S(1)}, f32[1,6,32,128]{3,1,2,0:T(8,128)S(1)}, u32[]{:S(2)}, u32[]{:S(2)}) collective-permute-start(f32[1,6,32,128]{3,1,2,0:T(8,128)S(1)} %get-tuple-element.104), channel_id=1, source_target_pairs={{16,0},{32,16},{48,32},{64,48},{80,64},{96,80},{112,96},{128,112},... | collective-permute-start | bytes 294920 | tf_op jit(solution)/shard_map/ppermute | solution.py:22
  181.2 14.4 %collective-permute-start.5 = (f32[1,6,32,128]{3,1,2,0:T(8,128)S(1)}, f32[1,6,32,128]{3,1,2,0:T(8,128)S(1)}, u32[]{:S(2)}, u32[]{:S(2)}) collective-permute-start(f32[1,6,32,128]{3,1,2,0:T(8,128)S(1)} %get-tuple-element.105), channel_id=1, source_target_pairs={{0,16},{16,32},{32,48},{48,64},{64,80},{80,96},{96,112},{112,128},... | collective-permute-start | bytes 294920 | tf_op jit(solution)/shard_map/ppermute | solution.py:21
  187.3 18.2 %all-to-all-start.5 = ((bf16[16,2,1,4096]{3,1,2,0:T(2,128)(2,1)}), bf16[16,2,1,4096]{3,1,2,0:T(2,128)(2,1)S(1)}, u32[]{:S(2)}, u32[]{:S(2)}) async-start(bf16[16,2,1,4096]{3,1,2,0:T(2,128)(2,1)} %reshape.2265), calls=%async_computation.5 | async-start | bytes 524288 | tf_op jit(solution)/shard_map/all_to_all | solution.py:157
  207.6 10.0 %copy-start.9 = (f32[1,28,30,128]{3,1,2,0:T(8,128)S(1)}, f32[1,28,30,128]{3,1,2,0:T(8,128)}, u32[]{:S(2)}) copy-start(f32[1,28,30,128]{3,1,2,0:T(8,128)} %get-tuple-element.32) | copy-start | bytes 1290244
  207.7 10.0 %copy-start.22 = (f32[1,28,4,128]{3,1,2,0:T(8,128)S(1)}, f32[1,28,4,128]{3,1,2,0:T(8,128)}, u32[]{:S(2)}) copy-start(f32[1,28,4,128]{3,1,2,0:T(8,128)} %get-tuple-element.22) | copy-start | bytes 172036
  208.8 19.2 %all-to-all-start.6 = ((bf16[16,2,1,4096]{3,1,2,0:T(2,128)(2,1)}), bf16[16,2,1,4096]{3,1,2,0:T(2,128)(2,1)S(1)}, u32[]{:S(2)}, u32[]{:S(2)}) async-start(bf16[16,2,1,4096]{3,1,2,0:T(2,128)(2,1)} %bitcast.162), calls=%async_computation.6 | async-start | bytes 524288 | tf_op jit(solution)/shard_map/all_to_all | solution.py:146
  220.6 10.8 %copy-start.3 = (f32[16,32,128]{2,1,0:T(8,128)S(1)}, f32[16,32,128]{2,1,0:T(8,128)}, u32[]{:S(2)}) copy-start(f32[16,32,128]{2,1,0:T(8,128)} %param.14) | copy-start | bytes 786436
  220.7 10.8 %copy-start.4 = (f32[1,16,32,128]{3,1,2,0:T(8,128)S(1)}, f32[1,16,32,128]{3,1,2,0:T(8,128)}, u32[]{:S(2)}) copy-start(f32[1,16,32,128]{3,1,2,0:T(8,128)} %get-tuple-element.8) | copy-start | bytes 786436
  220.7 10.8 %copy-start.16 = (f32[1,16,31,128]{3,1,2,0:T(8,128)S(1)}, f32[1,16,31,128]{3,1,2,0:T(8,128)}, u32[]{:S(2)}) copy-start(f32[1,16,31,128]{3,1,2,0:T(8,128)} %get-tuple-element.102) | copy-start | bytes 761860
  220.7 10.8 %copy-start.17 = (f32[1,16,31,128]{3,1,2,0:T(8,128)S(1)}, f32[1,16,31,128]{3,1,2,0:T(8,128)}, u32[]{:S(2)}) copy-start(f32[1,16,31,128]{3,1,2,0:T(8,128)} %get-tuple-element.103) | copy-start | bytes 761860
  220.7 10.8 %copy-start.18 = (f32[1,16,30,128]{3,1,2,0:T(8,128)S(1)}, f32[1,16,30,128]{3,1,2,0:T(8,128)}, u32[]{:S(2)}) copy-start(f32[1,16,30,128]{3,1,2,0:T(8,128)} %get-tuple-element.98) | copy-start | bytes 737284
  220.7 10.8 %copy-start.19 = (f32[1,16,30,128]{3,1,2,0:T(8,128)S(1)}, f32[1,16,30,128]{3,1,2,0:T(8,128)}, u32[]{:S(2)}) copy-start(f32[1,16,30,128]{3,1,2,0:T(8,128)} %get-tuple-element.99) | copy-start | bytes 737284
  220.7 10.8 %copy-start.26 = (f32[1,16,6,128]{3,1,2,0:T(8,128)S(1)}, f32[1,16,6,128]{3,1,2,0:T(8,128)}, u32[]{:S(2)}) copy-start(f32[1,16,6,128]{3,1,2,0:T(8,128)} %get-tuple-element.80) | copy-start | bytes 147460
  220.7 10.8 %copy-start.27 = (f32[1,16,6,128]{3,1,2,0:T(8,128)S(1)}, f32[1,16,6,128]{3,1,2,0:T(8,128)}, u32[]{:S(2)}) copy-start(f32[1,16,6,128]{3,1,2,0:T(8,128)} %get-tuple-element.81) | copy-start | bytes 147460
  220.7 10.8 %copy-start.32 = (f32[1,16,5,128]{3,1,2,0:T(8,128)S(1)}, f32[1,16,5,128]{3,1,2,0:T(8,128)}, u32[]{:S(2)}) copy-start(f32[1,16,5,128]{3,1,2,0:T(8,128)} %get-tuple-element.84) | copy-start | bytes 122884
  220.7 10.8 %copy-start.33 = (f32[1,16,4,128]{3,1,2,0:T(8,128)S(1)}, f32[1,16,4,128]{3,1,2,0:T(8,128)}, u32[]{:S(2)}) copy-start(f32[1,16,4,128]{3,1,2,0:T(8,128)} %get-tuple-element.88) | copy-start | bytes 98308
  220.7 10.8 %copy-start.36 = (f32[1,16,2,128]{3,1,2,0:T(8,128)S(1)}, f32[1,16,2,128]{3,1,2,0:T(8,128)}, u32[]{:S(2)}) copy-start(f32[1,16,2,128]{3,1,2,0:T(8,128)} %get-tuple-element.96) | copy-start | bytes 49156
  220.8 10.8 %copy-start.37 = (f32[1,16,1,128]{3,1,2,0:T(8,128)S(1)}, f32[1,16,1,128]{3,1,2,0:T(8,128)}, u32[]{:S(2)}) copy-start(f32[1,16,1,128]{3,1,2,0:T(8,128)} %get-tuple-element.100) | copy-start | bytes 24580
  (18 other events, 24.9 us)
Sparse Core Ops, SparseCore 0:
  31.4 37.5 all-gather.1
